TPU v7x, 512 devices: a whole 4x8x8 slice. The times are simulated.
512 devices in a mesh: dp: 8 (over x, core), expert: 64 (over z, y).
Axes of the slice: x: 4, y: 8, z: 8, core: 2. Of those that a mesh axis runs over, the one named last changes fastest.
Arguments:
- tokens: bfloat16 [65536, 512], P(('dp', 'expert')), may hold values from -6 to 6
- modality: int32 [65536], P(('dp', 'expert')), may hold values 0 or 1
- modal_gains: float32 [2, 512], replicated, may hold values from 0.5 to 2
- routes: int32 [65536, 2], P(('dp', 'expert')), may hold values from 0 to 63, all different within a row; in each aligned block of 128 rows (0 to 127, 128 to 255, ...) at most 8 rows name the same one
- gate_share: int32 [65536], P(('dp', 'expert')), may hold values from 1 to 15
- up_weight: bfloat16 [64, 2048, 512], P('expert', 'dp'), may hold values from -0.25 to 0.25
- down_weight: bfloat16 [64, 2048, 512], P('expert', 'dp'), may hold values from -0.125 to 0.125
- cotangent: bfloat16 [65536, 512], P(('dp', 'expert')), may hold values from -6 to 6
Outputs:
- moe_output: bfloat16 [65536, 512], P(('dp', 'expert'))
- token_grad: bfloat16 [65536, 512], P(('dp', 'expert'))
- up_grad: bfloat16 [64, 2048, 512], P('expert', 'dp')
- down_grad: bfloat16 [64, 2048, 512], P('expert', 'dp')
Inputs may be any that keep to these rules, and one draw needn't show every extreme that they name: `routes`: each row names two different experts; among the 128 rows of one device no expert is named more than 8 times, and in every draw some device names some expert exactly 8 times.
All inputs are finite; a program needn't handle non-finite values. No bound on the sum of `modality` on one device may be relied on, other than what follows from the above.
Results may differ from a plain program's by a relative error of at most 0.014.
Values may be sent and summed in bfloat16 or wider, within the bound.
No kernel may reach another device: no remote copies, remote signals or barrier semaphores. Data moves between devices by JAX's collectives and lax.ppermute only.
A program may use at most 64 MiB of HBM per device.

v0:
```python
import math
import jax
import jax.numpy as jnp
from jax import lax
from jax.sharding import PartitionSpec as P

root_half = 0.7071067811865476
density = 0.3989422804014327


def gelu_value(values):
    return values * 0.5 * (1.0 + lax.erf(values * root_half))


def gelu_slope(values):
    return (
        0.5 * (1.0 + lax.erf(values * root_half))
        + values * jnp.exp(-0.5 * values * values) * density
    )


def row_product(left_side, right_side, right_axis):
    numbers = (((1,), (right_axis,)), ((), ()))
    return lax.dot_general(left_side, right_side, numbers, preferred_element_type=jnp.float32)


def row_contract(left_side, right_side):
    numbers = (((0,), (0,)), ((), ()))
    return lax.dot_general(left_side, right_side, numbers, preferred_element_type=jnp.float32)


def on_device(tokens, modality, modal_gains, routes, gate_share, up_weight, down_weight, cotangent):
    tok_count = tokens.shape[0]
    model_width = tokens.shape[1]
    expert_count = lax.axis_size("expert")
    replica_count = lax.axis_size("x") * lax.axis_size("core")
    capacity = 4 * tok_count // expert_count
    slot_count = expert_count * capacity
    route_count = 2 * tok_count
    grad_scale = 1.0 / math.sqrt(2 * tok_count * replica_count)
    shard = jnp.concatenate([up_weight, down_weight], axis=0)
    whole = lax.all_gather(
        lax.all_gather(shard, "x", axis=1, tiled=True), "core", axis=1, tiled=True
    )
    whole_up, whole_down = (whole[0], whole[1])
    x_float = tokens.astype(jnp.float32)
    inv_rms = lax.rsqrt(jnp.mean(x_float * x_float, axis=-1, keepdims=True) + 1e-06)
    gain_rows = jnp.where(modality[:, None] == 1, modal_gains[1][None, :], modal_gains[0][None, :])
    normed = (x_float * inv_rms * gain_rows).astype(jnp.bfloat16)
    gate_first = gate_share.astype(jnp.float32) / 16.0
    flat_routes = routes.reshape(-1)
    one_hot = flat_routes[:, None] == jnp.arange(expert_count, dtype=jnp.int32)[None, :]
    route_ids = jnp.arange(route_count, dtype=jnp.int32)
    before = (route_ids[None, :] < route_ids[:, None]).astype(jnp.bfloat16)
    earlier = jnp.dot(before, one_hot.astype(jnp.bfloat16), preferred_element_type=jnp.float32)
    position = jnp.sum(jnp.where(one_hot, earlier, 0.0), axis=1).astype(jnp.int32)
    slot_index = (flat_routes * capacity + position).reshape(tok_count, 2)
    slot_ids = jnp.arange(slot_count, dtype=jnp.int32)[:, None]
    first_hit = slot_ids == slot_index[:, 0][None, :]
    second_hit = slot_ids == slot_index[:, 1][None, :]
    pick = (first_hit | second_hit).astype(jnp.bfloat16)
    weigh = jnp.where(
        first_hit, gate_first[None, :], jnp.where(second_hit, 1.0 - gate_first[None, :], 0.0)
    ).astype(jnp.bfloat16)
    pick = pick.reshape(expert_count, 1, capacity, tok_count)
    weigh = weigh.reshape(expert_count, 1, capacity, tok_count)
    blank = jnp.zeros_like(pick)
    gather_side = jnp.concatenate(
        [jnp.concatenate([pick, blank], axis=3), jnp.concatenate([blank, weigh], axis=3)], axis=1
    ).reshape(2 * slot_count, 2 * tok_count)
    return_side = jnp.concatenate(
        [jnp.concatenate([weigh, blank], axis=3), jnp.concatenate([blank, pick], axis=3)], axis=1
    ).reshape(2 * slot_count, 2 * tok_count)
    sources = jnp.concatenate([normed, cotangent], axis=0)
    sending = jnp.dot(gather_side, sources, preferred_element_type=jnp.float32).astype(jnp.bfloat16)
    arrived = lax.all_to_all(
        sending.reshape(expert_count, 2 * capacity, model_width),
        "expert",
        split_axis=0,
        concat_axis=0,
        tiled=True,
    )
    expert_rows = arrived[:, :capacity].reshape(slot_count, model_width)
    grad_rows = arrived[:, capacity:].reshape(slot_count, model_width)
    pre_act = row_product(expert_rows, whole_up, 1)
    activated = gelu_value(pre_act).astype(jnp.bfloat16)
    expert_out = row_product(activated, whole_down, 0).astype(jnp.bfloat16)
    hidden_grad = row_product(grad_rows, whole_down, 1)
    pre_grad = (hidden_grad * gelu_slope(pre_act)).astype(jnp.bfloat16)
    normed_part = row_product(pre_grad, whole_up, 0).astype(jnp.bfloat16)
    leaving = jnp.concatenate(
        [
            expert_out.reshape(expert_count, capacity, model_width),
            normed_part.reshape(expert_count, capacity, model_width),
        ],
        axis=1,
    )
    back = lax.all_to_all(leaving, "expert", split_axis=0, concat_axis=0, tiled=True)
    up_term = row_contract(pre_grad, expert_rows) * grad_scale
    down_term = row_contract(activated, grad_rows) * grad_scale
    parts = jnp.stack([up_term, down_term], axis=1).astype(jnp.bfloat16)
    grad_pair = lax.psum_scatter(
        lax.psum_scatter(parts, "core", scatter_dimension=0, tiled=True),
        "x",
        scatter_dimension=0,
        tiled=True,
    )
    up_grad = grad_pair[:, 0][None]
    down_grad = grad_pair[:, 1][None]
    combined = row_contract(return_side, back.reshape(2 * slot_count, model_width))
    moe_output = combined[:tok_count].astype(jnp.bfloat16)
    normed_grad = combined[tok_count:]
    scaled = gain_rows * normed_grad
    token_grad = (
        inv_rms * scaled - x_float * inv_rms**3 * jnp.mean(x_float * scaled, axis=-1, keepdims=True)
    ).astype(jnp.bfloat16)
    return (moe_output, token_grad, up_grad, down_grad)


def solution(mesh):
    dp_size, expert_size = mesh.devices.shape
    cores = 2
    mesh = jax.sharding.Mesh(
        mesh.devices.reshape(dp_size // cores, cores, expert_size), ("x", "core", "expert")
    )
    placed = (
        P(("x", "core", "expert"), None),
        P(("x", "core", "expert")),
        P(),
        P(("x", "core", "expert"), None),
        P(("x", "core", "expert")),
        P("expert", ("x", "core"), None),
        P("expert", ("x", "core"), None),
        P(("x", "core", "expert"), None),
    )
    return jax.shard_map(
        on_device,
        mesh=mesh,
        in_specs=placed,
        out_specs=(
            P(("x", "core", "expert"), None),
            P(("x", "core", "expert"), None),
            P("expert", ("x", "core"), None),
            P("expert", ("x", "core"), None),
        ),
        check_vma=False,
    )
```

profile of v0, /device:TPU:6, one launch (start us, length us, event | category | flops | bytes accessed | tf_op | source)
XLA Modules:
  0.0 178.2 jit_solution(408768301681310758)
XLA Ops:
  7.2 0.0 copy-start
  7.2 0.0 copy-start.5
  7.2 0.0 copy-start.2
  7.2 0.0 copy-start.1
  7.2 0.0 all-gather.3.cloned.1.call-start
  7.3 1.9 %pad_maximum_fusion.2 = bf16[2,256,512]{2,1,0:T(8,128)(2,1)} fusion(bf16[1,256,512]{2,1,0:T(8,128)(2,1)} %param.14, bf16[1,256,512]{2,1,0:T(8,128)(2,1)} %param.13), kind=kLoop, calls=%fused_computation.37 | loop fusion | flops 262144 | bytes 1048576 | tf_op jit(solution)/shard_map/concatenate | solution.py:41
  9.2 0.0 all-gather.3.cloned.1.call-update
  9.2 0.0 all-gather.5.cloned.1.call-start
  9.3 0.8 copy.18
  10.1 0.1 eq.88
  10.2 0.2 fusion.15
  10.4 0.1 convert_element_type.59
  10.6 0.1 copy.19
  10.6 0.7 convert_multiply_fusion.4
  11.3 0.7 multiply_add_fusion.1
  12.0 37.1 %all-gather.3.cloned.1.call-done = bf16[2,1024,512]{2,1,0:T(8,128)(2,1)} async-done(((bf16[2,256,512]{2,1,0:T(8,128)(2,1)}), bf16[2,1024,512]{2,1,0:T(8,128)(2,1)}) %all-gather.3.cloned.1.call-update) | async-done | bytes 2097168 | tf_op jit(solution)/shard_map/all_gather | solution.py:43
  49.1 0.0 all-gather.5.cloned.1.call-update
  49.1 0.0 reduce-scatter.3.cloned.1.call-start
  49.2 0.0 copy-done
  49.2 0.1 fusion.24
  49.3 0.1 fusion.32
  49.4 0.1 fusion.22
  49.6 0.1 fusion.21
  49.7 0.0 copy-done.5
  49.7 0.0 copy-done.2
  49.8 0.1 fusion.23
  49.9 0.0 copy-done.1
  49.9 0.4 convolution_convert_fusion
  50.3 42.9 %all_to_all.10 = bf16[64,16,512]{2,1,0:T(8,128)(2,1)S(1)} all-to-all(bf16[64,16,512]{2,1,0:T(8,128)(2,1)S(1)} %bitcast.57), channel_id=1, replica_groups=mesh['x'=4,'core'=2,'expert'=64] {'expert'}, dimensions={0} | all-to-all | bytes 2097152 | tf_op jit(solution)/shard_map/all_to_all | solution.py:76
  93.2 0.0 all-gather.5.cloned.1.call-done
  93.2 0.0 copy-start.3
  93.2 3.1 %multiply_convert_fusion.2 = (bf16[512,2048]{1,0:T(8,128)(2,1)S(1)}, f32[512,2048]{1,0:T(8,128)S(1)}) fusion(bf16[2,2048,512]{2,1,0:T(8,128)(2,1)} %all-gather.5.cloned.1.call-done, bf16[64,16,512]{2,1,0:T(8,128)(2,1)S(1)} %all_to_all.10), kind=kOutput, calls=%fused_computation.10 | convolution fusion | flops 1078984704 | bytes 8912896 | tf_op jit(solution)/shard_map/dot_general | solution.py:24
  96.3 0.0 copy-start.6
  96.3 0.0 copy-done.3
  96.3 2.8 %fusion.5 = bf16[512,2048]{1,0:T(8,128)(2,1)S(1)} fusion(f32[512,2048]{1,0:T(8,128)S(1)} %get-tuple-element.17, bf16[2,2048,512]{2,1,0:T(8,128)(2,1)S(1)} %copy-done.3, bf16[64,16,512]{2,1,0:T(8,128)(2,1)S(1)} %all_to_all.10), kind=kOutput, calls=%fused_computation.6 | convolution fusion | flops 1084227584 | bytes 8912896 | tf_op jit(solution)/shard_map/dot_general | solution.py:24
  99.1 0.0 copy-start.8
  99.1 0.0 copy-done.6
  99.2 1.3 fusion.7
  100.5 0.0 copy-done.8
  100.5 1.3 fusion.6
  101.8 2.3 %pad_maximum_fusion = bf16[2048,2,512]{2,0,1:T(8,128)(2,1)} fusion(bf16[2048,1,512]{2,0,1:T(8,128)(2,1)S(1)} %fusion.7, bf16[2048,1,512]{2,0,1:T(8,128)(2,1)S(1)} %fusion.6), kind=kLoop, calls=%fused_computation.7 | loop fusion | flops 2097152 | bytes 8388608 | tf_op jit(solution)/shard_map/stack | solution.py:101
  104.1 0.0 copy-start.9
  104.1 0.0 reduce-scatter.3.cloned.1.call-update
  104.2 0.0 reduce-scatter.5.cloned.1.call-start
  104.2 15.5 %reduce-scatter.3.cloned.1.call-done = bf16[1024,2,512]{2,0,1:T(8,128)(2,1)} async-done(((bf16[2048,2,512]{2,0,1:T(8,128)(2,1)}), bf16[1024,2,512]{2,0,1:T(8,128)(2,1)}) %reduce-scatter.3.cloned.1.call-update) | async-done | bytes 2097168 | tf_op jit(solution)/shard_map/reduce_scatter | solution.py:103
  119.7 0.0 reduce-scatter.5.cloned.1.call-update
  119.7 0.0 copy-done.9
  119.7 0.0 copy-start.4
  119.7 0.0 copy-start.7
  119.8 3.0 %fusion.13 = bf16[64,8,512]{2,1,0:T(8,128)(2,1)S(1)} fusion(bf16[512,2048]{1,0:T(8,128)(2,1)S(1)} %copy-done.9, bf16[2,2048,512]{2,1,0:T(8,128)(2,1)} %all-gather.5.cloned.1.call-done), kind=kOutput, calls=%fused_computation.22 | convolution fusion | flops 1074003968 | bytes 4718592 | tf_op jit(solution)/shard_map/dot_general | solution.py:24
  122.8 0.0 copy-done.4
  122.8 0.5 copy-done.7
  123.2 1.2 fusion.14
  124.5 0.1 pad_maximum_fusion.1
  124.6 43.0 %all_to_all.11 = bf16[64,16,512]{2,1,0:T(8,128)(2,1)S(1)} all-to-all(bf16[64,16,512]{2,1,0:T(8,128)(2,1)S(1)} %pad_maximum_fusion.1), channel_id=1, replica_groups=mesh['x'=4,'core'=2,'expert'=64] {'expert'}, dimensions={0} | all-to-all | bytes 2097152 | tf_op jit(solution)/shard_map/all_to_all | solution.py:98
  167.6 0.4 fusion.36
  168.1 0.7 slice.87
  168.8 0.2 fusion.28
  169.0 0.8 fusion.27
  169.8 0.0 reduce-scatter.5.cloned.1.call-done
  169.8 1.9 %slice_bitcast_fusion.20 = (bf16[1,256,512]{2,1,0:T(8,128)(2,1)}, bf16[1,256,512]{2,1,0:T(8,128)(2,1)}) fusion(bf16[256,2,512]{2,0,1:T(8,128)(2,1)} %reduce-scatter.5.cloned.1.call-done), kind=kLoop, calls=%fused_computation.54 | loop fusion | bytes 1048576 | tf_op jit(solution)/shard_map/broadcast_in_dim;squeeze | solution.py:109
  (7 shorter events, 0.0 us)
Async XLA Ops:
  7.2 42.0 %copy-start = (bf16[128,512]{1,0:T(8,128)(2,1)S(1)}, bf16[128,512]{1,0:T(8,128)(2,1)}, u32[]{:S(2)}) copy-start(bf16[128,512]{1,0:T(8,128)(2,1)} %param.8) | copy-start | bytes 393220
  7.2 42.5 %copy-start.5 = (s32[128]{0:T(128)S(1)}, s32[128]{0:T(128)}, u32[]{:S(2)}) copy-start(s32[128]{0:T(128)} %param.9) | copy-start | bytes 1540
  7.2 42.6 %copy-start.2 = (f32[2,512]{1,0:T(2,128)S(1)}, f32[2,512]{1,0:T(2,128)}, u32[]{:S(2)}) copy-start(f32[2,512]{1,0:T(2,128)} %param.10) | copy-start | bytes 12292
  7.2 42.7 %copy-start.1 = (bf16[128,512]{1,0:T(8,128)(2,1)S(1)}, bf16[128,512]{1,0:T(8,128)(2,1)}, u32[]{:S(2)}) copy-start(bf16[128,512]{1,0:T(8,128)(2,1)} %param.15) | copy-start | bytes 393220
  7.2 41.9 %all-gather.3.cloned.1.call-start = ((), (), s32[]{:S(2)}) async-start(), calls=%async_computation.4 | async-start | bytes 2621440 | tf_op jit(solution)/shard_map/all_gather | solution.py:43
  9.2 84.0 %all-gather.5.cloned.1.call-start = ((), (), s32[]{:S(2)}) async-start(), calls=%async_computation.5 | async-start | bytes 6291456 | tf_op jit(solution)/shard_map/all_gather | solution.py:42
  49.1 70.6 %reduce-scatter.3.cloned.1.call-start = ((), (), s32[]{:S(2)}) async-start(), calls=%async_computation.6 | async-start | bytes 6291456 | tf_op jit(solution)/shard_map/reduce_scatter | solution.py:103
  93.2 3.1 %copy-start.3 = (bf16[2,2048,512]{2,1,0:T(8,128)(2,1)S(1)}, bf16[2,2048,512]{2,1,0:T(8,128)(2,1)}, u32[]{:S(2)}) copy-start(bf16[2,2048,512]{2,1,0:T(8,128)(2,1)} %all-gather.5.cloned.1.call-done) | copy-start | bytes 12582916
  96.3 2.9 %copy-start.6 = (bf16[512,2048]{1,0:T(8,128)(2,1)}, bf16[512,2048]{1,0:T(8,128)(2,1)S(1)}, u32[]{:S(2)}) copy-start(bf16[512,2048]{1,0:T(8,128)(2,1)S(1)} %get-tuple-element.16) | copy-start | bytes 6291460
  99.1 1.3 copy-start.8
  104.1 15.6 %copy-start.9 = (bf16[512,2048]{1,0:T(8,128)(2,1)S(1)}, bf16[512,2048]{1,0:T(8,128)(2,1)}, u32[]{:S(2)}) copy-start(bf16[512,2048]{1,0:T(8,128)(2,1)} %copy-done.8) | copy-start | bytes 6291460
  104.2 65.6 %reduce-scatter.5.cloned.1.call-start = ((), (), s32[]{:S(2)}) async-start(), calls=%async_computation.7 | async-start | bytes 2621440 | tf_op jit(solution)/shard_map/reduce_scatter | solution.py:102
  119.7 3.0 %copy-start.4 = (bf16[2,2048,512]{2,1,0:T(8,128)(2,1)S(1)}, bf16[2,2048,512]{2,1,0:T(8,128)(2,1)}, u32[]{:S(2)}) copy-start(bf16[2,2048,512]{2,1,0:T(8,128)(2,1)} %all-gather.5.cloned.1.call-done) | copy-start | bytes 12582916
  119.7 3.5 %copy-start.7 = (bf16[512,2048]{1,0:T(8,128)(2,1)S(1)}, bf16[512,2048]{1,0:T(8,128)(2,1)}, u32[]{:S(2)}) copy-start(bf16[512,2048]{1,0:T(8,128)(2,1)} %copy-done.6) | copy-start | bytes 6291460
Sparse Core Ops, SparseCore 0:
  10.1 38.8 all-gather.2
  51.2 23.7 all-gather.4
  104.3 15.3 reduce-scatter.2
  122.6 34.4 reduce-scatter.4
where the time goes:
time: 178 us
  blocking collectives  85.9 us (48%)
  waiting for transfers between devices  52.6 us (30%)
  between operations  14.1 us (8%)
  matrix products  13.9 us (8%)
  other arithmetic  7.37 us (4%)
  local copies, waits for them, and re-layouts  4.15 us (2%)
    all_to_all x1, blocking collectives, on_device(): lax.all_to_all(leaving, 'expert', split_axis=0, concat_axis=0, tiled=True)  43 us
    all_to_all x1, blocking collectives, on_device(): lax.all_to_all(sending.reshape(expert_count, 2 * capacity, model_width),...  42.9 us
    all_gather x1, waiting for transfers between devices, on_device(): lax.all_gather(shard, 'x', axis=1, tiled=True)  37.1 us
    reduce_scatter x1, waiting for transfers between devices, on_device(): lax.psum_scatter(parts, 'core', scatter_dimension=0, tiled=True)  15.5 us
    dot_general x4, matrix products, row_product(): lax.dot_general(left_side, right_side, numbers, preferred_element_type=jn...  10.1 us
  transfers between devices with their start and end apart: 4, of which 2 were waited for; matrix products, arithmetic and copies ran while one was open for 6% of the time, Pallas kernels for 0%

commit v1 on v0

--- a/solution.py
+++ b/solution.py
@@ -6,6 +6,13 @@
 
 root_half = 0.7071067811865476
 density = 0.3989422804014327
+
+
+def register_patch(z):
+    passed = jnp.concatenate(
+        lax.all_to_all(jnp.stack(lax.axis_size("x") * [z], axis=0), "x", 0, 0), 1
+    )
+    return passed
 
 
 def gelu_value(values):
@@ -39,9 +46,7 @@
     route_count = 2 * tok_count
     grad_scale = 1.0 / math.sqrt(2 * tok_count * replica_count)
     shard = jnp.concatenate([up_weight, down_weight], axis=0)
-    whole = lax.all_gather(
-        lax.all_gather(shard, "x", axis=1, tiled=True), "core", axis=1, tiled=True
-    )
+    whole = lax.all_gather(register_patch(shard), "core", axis=1, tiled=True)
     whole_up, whole_down = (whole[0], whole[1])
     x_float = tokens.astype(jnp.float32)
     inv_rms = lax.rsqrt(jnp.mean(x_float * x_float, axis=-1, keepdims=True) + 1e-06)

time: 178 us -> 171 us (0.961)
  waiting for transfers between devices: 52.6 us -> 33.4 us
  starting transfers between devices: 0.16 us -> 9.52 us
  local copies, waits for them, and re-layouts: 4.15 us -> 6.59 us
  other arithmetic: 7.37 us -> 5.17 us
  blocking collectives: 85.9 us -> 88.1 us
    all_gather x2 -> x1, waiting for transfers between devices: 37.1 us -> 0.01 us  [on_device(): whole = lax.all_gather(register_patch(shard), 'core', axis=1, tiled=True)]
    all_to_all x0 -> x1, waiting for transfers between devices: none -> 18.8 us  [register_patch(): lax.all_to_all(jnp.stack(lax.axis_size('x') * [z], axis=0), 'x', 0, 0)]
    all_to_all x0 -> x1, starting transfers between devices: none -> 9.43 us  [register_patch(): lax.all_to_all(jnp.stack(lax.axis_size('x') * [z], axis=0), 'x', 0, 0)]
    all_to_all x1, blocking collectives: 42.9 us -> 45 us  [on_device(): lax.all_to_all(sending.reshape(expert_count, 2 * capacity, model_width),...]
  transfers between devices with their start and end apart: 4 -> 4, of which waited for: 2 -> 2; matrix products, arithmetic and copies ran while one was open for 6% -> 5% of each run, Pallas kernels for 0% -> 0%
where the time goes in v1:
time: 171 us
  blocking collectives  88.1 us (52%)
  waiting for transfers between devices  33.4 us (20%)
  between operations  14.1 us (8%)
  matrix products  13.9 us (8%)
  starting transfers between devices  9.52 us (6%)
  local copies, waits for them, and re-layouts  6.59 us (4%)
  other arithmetic  5.17 us (3%)
    all_to_all x1, blocking collectives, on_device(): lax.all_to_all(sending.reshape(expert_count, 2 * capacity, model_width),...  45 us
    all_to_all x1, blocking collectives, on_device(): lax.all_to_all(leaving, 'expert', split_axis=0, concat_axis=0, tiled=True)  43.1 us
    all_to_all x1, waiting for transfers between devices, register_patch(): lax.all_to_all(jnp.stack(lax.axis_size('x') * [z], axis=0), 'x', 0, 0)  18.8 us
    reduce_scatter x1, waiting for transfers between devices, on_device(): lax.psum_scatter(parts, 'core', scatter_dimension=0, tiled=True)  14.5 us
    dot_general x4, matrix products, row_product(): lax.dot_general(left_side, right_side, numbers, preferred_element_type=jn...  10.1 us
    all_to_all x1, starting transfers between devices, register_patch(): lax.all_to_all(jnp.stack(lax.axis_size('x') * [z], axis=0), 'x', 0, 0)  9.43 us
  transfers between devices with their start and end apart: 4, of which 2 were waited for; matrix products, arithmetic and copies ran while one was open for 5% of the time, Pallas kernels for 0%

profile of v1, /device:TPU:6, one launch (start us, length us, event | category | flops | bytes accessed | tf_op | source)
XLA Modules:
  0.0 170.7 jit_solution(7470323636594946946)
XLA Ops:
  7.2 0.0 copy-start.2
  7.2 0.0 copy-start.6
  7.2 1.1 pad_maximum_fusion.2
  8.3 1.5 stack.19
  9.8 9.4 %all-to-all-start.1 = ((bf16[4,2,256,512]{3,2,1,0:T(8,128)(2,1)}), bf16[4,2,256,512]{3,2,1,0:T(8,128)(2,1)S(1)}, u32[]{:S(2)}, u32[]{:S(2)}) async-start(bf16[4,2,256,512]{3,2,1,0:T(8,128)(2,1)} %stack.19), calls=%async_computation.1 | async-start | bytes 4194304 | tf_op jit(solution)/shard_map/all_to_all | solution.py:13
  19.2 0.0 copy-start
  19.2 0.0 all-gather.2.cloned.1.call-start
  19.2 0.0 copy-done.2
  19.2 0.1 copy.22
  19.3 0.1 eq.88
  19.5 0.0 copy-start.7
  19.5 0.0 copy-start.3
  19.5 0.2 fusion.15
  19.7 0.1 convert_element_type.59
  19.9 0.1 copy.23
  19.9 0.0 copy-done.6
  20.0 0.0 copy-start.1
  20.0 18.8 %all-to-all-done.1 = bf16[4,2,256,512]{3,2,1,0:T(8,128)(2,1)S(1)} async-done(((bf16[4,2,256,512]{3,2,1,0:T(8,128)(2,1)}), bf16[4,2,256,512]{3,2,1,0:T(8,128)(2,1)S(1)}, u32[]{:S(2)}, u32[]{:S(2)}) %all-to-all-start.1) | async-done | bytes 2097184 | tf_op jit(solution)/shard_map/all_to_all | solution.py:13
  38.8 1.6 copy.24
  40.4 0.0 all-gather.2.cloned.1.call-update
  40.4 0.0 reduce-scatter.3.cloned.1.call-start
  40.5 0.0 copy-done
  40.5 0.1 fusion.24
  40.6 0.1 fusion.32
  40.8 0.1 fusion.22
  40.9 0.1 fusion.21
  41.0 0.0 copy-done.7
  41.1 0.0 copy-done.3
  41.1 0.1 fusion.23
  41.2 0.0 copy-done.1
  41.2 0.4 convolution_convert_fusion
  41.6 45.0 %all_to_all.15 = bf16[64,16,512]{2,1,0:T(8,128)(2,1)S(1)} all-to-all(bf16[64,16,512]{2,1,0:T(8,128)(2,1)S(1)} %bitcast.61), channel_id=1, replica_groups=mesh['x'=4,'core'=2,'expert'=64] {'expert'}, dimensions={0} | all-to-all | bytes 2097152 | tf_op jit(solution)/shard_map/all_to_all | solution.py:81
  86.7 0.0 all-gather.2.cloned.1.call-done
  86.7 0.0 copy-start.4
  86.7 3.1 %multiply_convert_fusion.2 = (bf16[512,2048]{1,0:T(8,128)(2,1)S(1)}, f32[512,2048]{1,0:T(8,128)S(1)}) fusion(bf16[2,2048,512]{2,1,0:T(8,128)(2,1)} %all-gather.2.cloned.1.call-done, bf16[64,16,512]{2,1,0:T(8,128)(2,1)S(1)} %all_to_all.15), kind=kOutput, calls=%fused_computation.10 | convolution fusion | flops 1078984704 | bytes 8912896 | tf_op jit(solution)/shard_map/dot_general | solution.py:31
  89.7 0.0 copy-start.8
  89.8 0.0 copy-done.4
  89.8 2.8 %fusion.5 = bf16[512,2048]{1,0:T(8,128)(2,1)S(1)} fusion(f32[512,2048]{1,0:T(8,128)S(1)} %get-tuple-element.17, bf16[2,2048,512]{2,1,0:T(8,128)(2,1)S(1)} %copy-done.4, bf16[64,16,512]{2,1,0:T(8,128)(2,1)S(1)} %all_to_all.15), kind=kOutput, calls=%fused_computation.6 | convolution fusion | flops 1084227584 | bytes 8912896 | tf_op jit(solution)/shard_map/dot_general | solution.py:31
  92.6 0.0 copy-start.10
  92.6 0.0 copy-done.8
  92.6 1.3 fusion.7
  93.9 0.0 copy-done.10
  93.9 1.3 fusion.6
  95.3 2.3 %pad_maximum_fusion = bf16[2048,2,512]{2,0,1:T(8,128)(2,1)} fusion(bf16[2048,1,512]{2,0,1:T(8,128)(2,1)S(1)} %fusion.7, bf16[2048,1,512]{2,0,1:T(8,128)(2,1)S(1)} %fusion.6), kind=kLoop, calls=%fused_computation.7 | loop fusion | flops 2097152 | bytes 8388608 | tf_op jit(solution)/shard_map/stack | solution.py:106
  97.6 0.0 copy-start.11
  97.6 0.0 reduce-scatter.3.cloned.1.call-update
  97.6 0.0 reduce-scatter.5.cloned.1.call-start
  97.7 14.5 %reduce-scatter.3.cloned.1.call-done = bf16[1024,2,512]{2,0,1:T(8,128)(2,1)} async-done(((bf16[2048,2,512]{2,0,1:T(8,128)(2,1)}), bf16[1024,2,512]{2,0,1:T(8,128)(2,1)}) %reduce-scatter.3.cloned.1.call-update) | async-done | bytes 2097168 | tf_op jit(solution)/shard_map/reduce_scatter | solution.py:108
  112.1 0.0 reduce-scatter.5.cloned.1.call-update
  112.2 0.0 copy-done.11
  112.2 0.0 copy-start.5
  112.2 0.0 copy-start.9
  112.2 3.0 %fusion.13 = bf16[64,8,512]{2,1,0:T(8,128)(2,1)S(1)} fusion(bf16[512,2048]{1,0:T(8,128)(2,1)S(1)} %copy-done.11, bf16[2,2048,512]{2,1,0:T(8,128)(2,1)} %all-gather.2.cloned.1.call-done), kind=kOutput, calls=%fused_computation.22 | convolution fusion | flops 1074003968 | bytes 4718592 | tf_op jit(solution)/shard_map/dot_general | solution.py:31
  115.2 0.0 copy-done.5
  115.2 0.5 copy-done.9
  115.7 1.2 fusion.14
  116.9 0.1 pad_maximum_fusion.1
  117.0 43.1 %all_to_all.16 = bf16[64,16,512]{2,1,0:T(8,128)(2,1)S(1)} all-to-all(bf16[64,16,512]{2,1,0:T(8,128)(2,1)S(1)} %pad_maximum_fusion.1), channel_id=1, replica_groups=mesh['x'=4,'core'=2,'expert'=64] {'expert'}, dimensions={0} | all-to-all | bytes 2097152 | tf_op jit(solution)/shard_map/all_to_all | solution.py:103
  160.1 0.4 fusion.36
  160.6 0.7 slice.87
  161.3 0.2 fusion.28
  161.5 0.8 fusion.27
  162.3 0.0 reduce-scatter.5.cloned.1.call-done
  162.3 1.9 %slice_bitcast_fusion.20 = (bf16[1,256,512]{2,1,0:T(8,128)(2,1)}, bf16[1,256,512]{2,1,0:T(8,128)(2,1)}) fusion(bf16[256,2,512]{2,0,1:T(8,128)(2,1)} %reduce-scatter.5.cloned.1.call-done), kind=kLoop, calls=%fused_computation.54 | loop fusion | bytes 1048576 | tf_op jit(solution)/shard_map/broadcast_in_dim;squeeze | solution.py:114
  (9 shorter events, 0.1 us)
Async XLA Ops:
  7.2 12.1 %copy-start.2 = (s32[128,2]{0,1:T(2,128)S(1)}, s32[128,2]{0,1:T(2,128)}, u32[]{:S(2)}) copy-start(s32[128,2]{0,1:T(2,128)} %param.11) | copy-start | bytes 3076
  7.2 12.8 %copy-start.6 = (s32[128]{0:T(128)S(1)}, s32[128]{0:T(128)}, u32[]{:S(2)}) copy-start(s32[128]{0:T(128)} %param.12) | copy-start | bytes 1540
  9.8 29.0 %all-to-all-start.1 = ((bf16[4,2,256,512]{3,2,1,0:T(8,128)(2,1)}), bf16[4,2,256,512]{3,2,1,0:T(8,128)(2,1)S(1)}, u32[]{:S(2)}, u32[]{:S(2)}) async-start(bf16[4,2,256,512]{3,2,1,0:T(8,128)(2,1)} %stack.19), calls=%async_computation.1 | async-start | bytes 4194304 | tf_op jit(solution)/shard_map/all_to_all | solution.py:13
  19.2 21.3 %copy-start = (bf16[128,512]{1,0:T(8,128)(2,1)S(1)}, bf16[128,512]{1,0:T(8,128)(2,1)}, u32[]{:S(2)}) copy-start(bf16[128,512]{1,0:T(8,128)(2,1)} %param.8) | copy-start | bytes 393220
  19.2 67.4 %all-gather.2.cloned.1.call-start = ((), (), s32[]{:S(2)}) async-start(), calls=%async_computation.5 | async-start | bytes 6291456 | tf_op jit(solution)/shard_map/all_gather | solution.py:49
  19.5 21.5 %copy-start.7 = (s32[128]{0:T(128)S(1)}, s32[128]{0:T(128)}, u32[]{:S(2)}) copy-start(s32[128]{0:T(128)} %param.9) | copy-start | bytes 1540
  19.5 21.6 %copy-start.3 = (f32[2,512]{1,0:T(2,128)S(1)}, f32[2,512]{1,0:T(2,128)}, u32[]{:S(2)}) copy-start(f32[2,512]{1,0:T(2,128)} %param.10) | copy-start | bytes 12292
  20.0 21.2 %copy-start.1 = (bf16[128,512]{1,0:T(8,128)(2,1)S(1)}, bf16[128,512]{1,0:T(8,128)(2,1)}, u32[]{:S(2)}) copy-start(bf16[128,512]{1,0:T(8,128)(2,1)} %param.15) | copy-start | bytes 393220
  40.4 71.7 %reduce-scatter.3.cloned.1.call-start = ((), (), s32[]{:S(2)}) async-start(), calls=%async_computation.6 | async-start | bytes 6291456 | tf_op jit(solution)/shard_map/reduce_scatter | solution.py:108
  86.7 3.1 %copy-start.4 = (bf16[2,2048,512]{2,1,0:T(8,128)(2,1)S(1)}, bf16[2,2048,512]{2,1,0:T(8,128)(2,1)}, u32[]{:S(2)}) copy-start(bf16[2,2048,512]{2,1,0:T(8,128)(2,1)} %all-gather.2.cloned.1.call-done) | copy-start | bytes 12582916
  89.7 2.9 %copy-start.8 = (bf16[512,2048]{1,0:T(8,128)(2,1)}, bf16[512,2048]{1,0:T(8,128)(2,1)S(1)}, u32[]{:S(2)}) copy-start(bf16[512,2048]{1,0:T(8,128)(2,1)S(1)} %get-tuple-element.16) | copy-start | bytes 6291460
  92.6 1.3 copy-start.10
  97.6 14.6 %copy-start.11 = (bf16[512,2048]{1,0:T(8,128)(2,1)S(1)}, bf16[512,2048]{1,0:T(8,128)(2,1)}, u32[]{:S(2)}) copy-start(bf16[512,2048]{1,0:T(8,128)(2,1)} %copy-done.10) | copy-start | bytes 6291460
  97.6 64.7 %reduce-scatter.5.cloned.1.call-start = ((), (), s32[]{:S(2)}) async-start(), calls=%async_computation.7 | async-start | bytes 2621440 | tf_op jit(solution)/shard_map/reduce_scatter | solution.py:107
  112.2 3.0 %copy-start.5 = (bf16[2,2048,512]{2,1,0:T(8,128)(2,1)S(1)}, bf16[2,2048,512]{2,1,0:T(8,128)(2,1)}, u32[]{:S(2)}) copy-start(bf16[2,2048,512]{2,1,0:T(8,128)(2,1)} %all-gather.2.cloned.1.call-done) | copy-start | bytes 12582916
  112.2 3.5 %copy-start.9 = (bf16[512,2048]{1,0:T(8,128)(2,1)S(1)}, bf16[512,2048]{1,0:T(8,128)(2,1)}, u32[]{:S(2)}) copy-start(bf16[512,2048]{1,0:T(8,128)(2,1)} %copy-done.8) | copy-start | bytes 6291460
Sparse Core Ops, SparseCore 0:
  40.5 26.1 all-gather.1
  97.7 14.3 reduce-scatter.2
  115.2 34.4 reduce-scatter.4
